TPU v7x, 256 devices: a whole 4x4x8 slice. The times are simulated.
256 devices in a mesh: tm: 64 (over y, z, core), state: 4 (over x).
Axes of the slice: x: 4, y: 4, z: 8, core: 2. Of those that a mesh axis runs over, the one named last changes fastest.
Arguments:
- dynamics: float32 [512, 512], P('state'), may hold values from -1 to 1
- pattern: int32 [4, 4], replicated, may hold values from 0 to 1
- initial_mean: float32 [4, 512], replicated, may hold values from -6 to 6
- observed: float32 [1024, 4], P('tm'), may hold values from -6 to 6
- obs_index: int32 [1024], P('tm'), may hold values from 0 to 511
- obs_noise: float32 [1024], P('tm'), may hold values from 0.5 to 4
Outputs:
- filtered: float32 [1024, 4, 512], P('tm', 'state')
- smoothed: float32 [1024, 4, 512], P('tm', 'state')
All inputs are finite; a program needn't handle non-finite values.
Results may differ from a plain program's by a relative error of at most 0.0003.
Values sent between devices are 32-bit elements; how exact they have to be, the bound alone decides.
No kernel may reach another device: no remote copies, remote signals or barrier semaphores. Data moves between devices by JAX's collectives and lax.ppermute only.
A program may use at most 256 MiB of HBM per device.

v0:
```python
import jax
import jax.numpy as jnp
from jax import lax
from jax.sharding import PartitionSpec as P


def passed_along(block, axis, distance):
    devices = range(lax.axis_size(axis))
    route = [(i - distance, i) for i in devices if i - distance in devices]
    return lax.ppermute(block, axis, route)


def product(left, right):
    return jnp.dot(left, right, precision=lax.Precision.HIGHEST, preferred_element_type=jnp.float32)


def transposed(left, right):
    return lax.dot_general(
        left,
        right,
        (((1,), (1,)), ((), ())),
        precision=lax.Precision.HIGHEST,
        preferred_element_type=jnp.float32,
    )


def select_tree(usable, first_tree, second_tree):

    def select_leaf(first_leaf, second_leaf):
        return jnp.where(usable, first_leaf, second_leaf)

    return jax.tree.map(select_leaf, first_tree, second_tree)


def per_device(dynamics, pattern, initial_mean, observed, obs_index, obs_noise):
    row_count = dynamics.shape[0]
    state_width = dynamics.shape[1]
    blocks = pattern.shape[0]
    block_span = state_width // blocks
    seq_total = initial_mean.shape[0]
    steps_here = observed.shape[0]
    members = lax.axis_size("state")
    member = lax.axis_index("state")
    segments = lax.axis_size("tm")
    segment = lax.axis_index("tm")
    batch_here = seq_total // members
    present = jnp.maximum(pattern, jnp.eye(blocks, dtype=jnp.int32))
    block_mask = jnp.repeat(jnp.repeat(present, block_span, 0), block_span, 1).astype(jnp.float32)
    transition = lax.all_gather(dynamics, "state", axis=0, tiled=True) * block_mask
    kalman_gains = 1.0 / (1.0 + obs_noise)
    state_index = jnp.arange(state_width, dtype=jnp.int32)
    observed_masks = (state_index[None, :] == obs_index[:, None]).astype(jnp.float32)
    scale_factors = 1.0 - kalman_gains[:, None] * observed_masks
    final_local = jnp.arange(steps_here, dtype=jnp.int32) == steps_here - 1
    retain_flags = 1.0 - jnp.where((segment == segments - 1) & final_local, 1.0, 0.0).astype(
        jnp.float32
    )
    first_row = member * row_count
    owned_rows = (
        jnp.arange(row_count, dtype=jnp.int32)[:, None] + first_row == state_index[None, :]
    ).astype(jnp.float32)
    batch_start = member * batch_here
    local_observations = lax.dynamic_slice_in_dim(observed, batch_start, batch_here, 1)

    def combine_rows(earlier_full, later):
        return (
            product(later[0], earlier_full[0]),
            transposed(earlier_full[1], later[0]) + later[1],
        )

    def doubling(element, direction):
        identity = (owned_rows, jnp.zeros((seq_total, row_count), jnp.float32))
        distances = [1]
        for level_turn in range(9):
            if 2**level_turn < segments:
                distances.append(2**level_turn)
        current = element
        for level_turn, distance in enumerate(distances):
            arrived = passed_along(current, "tm", direction * distance)
            if direction > 0:
                usable = segment >= distance
            else:
                usable = segment + distance < segments
            if level_turn == 0:
                current = select_tree(usable, arrived, identity)
            else:
                gathered = (
                    lax.all_gather(arrived[0], "state", axis=0, tiled=True),
                    lax.all_gather(arrived[1], "state", axis=1, tiled=True),
                )
                current = select_tree(usable, combine_rows(gathered, current), current)
        return current

    def entering(element, start_mean, direction):
        map_rows, map_offsets = doubling(element, direction)
        if start_mean is None:
            entry_rows = map_offsets
        else:
            entry_rows = map_offsets + transposed(start_mean, map_rows)
        return lax.all_to_all(entry_rows, "state", split_axis=0, concat_axis=1, tiled=True)

    def filter_portion(carried, inputs):
        row_block, offsets = carried
        hit_mask, scaling, gain_now, obs_now = inputs
        column_now = product(row_block, hit_mask)
        offsets = offsets + gain_now * obs_now[:, None] * column_now[None, :]
        row_block = product(row_block * scaling[None, :], transition)
        return ((row_block, offsets), None)

    initial_shifts = jnp.zeros((seq_total, row_count), jnp.float32)
    (filter_rows, filter_offsets), unused_value = lax.scan(
        filter_portion,
        (owned_rows, initial_shifts),
        (observed_masks, scale_factors, kalman_gains, observed),
        reverse=True,
    )
    filter_input = entering((filter_rows, filter_offsets), initial_mean, 1)

    def forward_sweep(current_state, inputs):
        scaling, hit_mask, gain_now, obs_now = inputs
        current_state = (
            transposed(current_state, transition) * scaling[None, :]
            + gain_now * obs_now[:, None] * hit_mask[None, :]
        )
        return (current_state, current_state)

    unused_value, filtered = lax.scan(
        forward_sweep,
        filter_input,
        (scale_factors, observed_masks, kalman_gains, local_observations),
    )
    flat_means = filtered.reshape(steps_here * batch_here, state_width)
    backward_mapped = product(transposed(flat_means, transition), transition).reshape(
        steps_here, batch_here, state_width
    )
    residual_terms = (
        filtered - retain_flags[:, None, None] * backward_mapped * scale_factors[:, None, :]
    )

    def smoother_update(current_state, inputs):
        scaling, keep_flag, gap_term = inputs
        current_state = keep_flag * product(current_state, transition) * scaling[None, :] + gap_term
        return (current_state, current_state)

    zero_portion = jnp.zeros((batch_here, state_width), jnp.float32)
    local_shifts, unused_value = lax.scan(
        smoother_update, zero_portion, (scale_factors, retain_flags, residual_terms), reverse=True
    )
    smooth_offsets = lax.all_to_all(local_shifts, "state", split_axis=1, concat_axis=0, tiled=True)

    def smoother_portion(row_block, inputs):
        scaling, keep_flag = inputs
        return (keep_flag * transposed(row_block * scaling[None, :], transition), None)

    smoother_rows, unused_value = lax.scan(
        smoother_portion, owned_rows, (scale_factors, retain_flags)
    )
    smoother_input = entering((smoother_rows, smooth_offsets), None, -1)
    unused_value, smoothed = lax.scan(
        smoother_update, smoother_input, (scale_factors, retain_flags, residual_terms), reverse=True
    )
    return (filtered, smoothed)


def solution(mesh):
    return jax.shard_map(
        per_device,
        mesh=mesh,
        in_specs=(P("state", None), P(), P(), P("tm", None), P("tm"), P("tm")),
        out_specs=(P("tm", "state", None), P("tm", "state", None)),
        check_vma=False,
    )
```

profile of v0, /device:TPU:8, one launch (start us, length us, event | category | flops | bytes accessed | tf_op | source)
XLA Modules:
  0.0 767.9 jit_solution(12369168793150731097)
XLA Ops:
  10.4 29.0 %all-gather.13.cloned.1.call-done = f32[512,512]{1,0:T(8,128)} async-done(((f32[128,512]{1,0:T(8,128)}), f32[512,512]{1,0:T(8,128)}) %all-gather.13.cloned.1.call-update) | async-done | bytes 1048592 | tf_op jit(solution)/shard_map/all_gather | solution.py:49
  40.8 40.3 %while.71 = (s32[]{:T(128)}, f32[128,512]{1,0:T(8,128)S(1)}, f32[16]{0:T(128)S(1)}, f32[16,512]{1,0:T(8,128)S(1)}, f32[512,512]{1,0:T(8,128)S(1)}, /*index=5*/s32[]{:T(128)}) while((s32[]{:T(128)}, f32[128,512]{1,0:T(8,128)S(1)}, f32[16]{0:T(128)S(1)}, f32[16,512]{1,0:T(8,128)S(1)}, f32[512,512]{1,0:T(8,128)S(1)}, /*index=5*/s32[]{:T(128)}) %tuple.143), condition=%wide.region_7.8_spmd, body=%wide.region_6.7_spmd.sunk | while | flops 402784256 | bytes 2103393 | solution.py:155
  83.7 38.8 %while.73 = (s32[]{:T(128)}, f32[128,512]{1,0:T(8,128)S(1)}, f32[4,128]{1,0:T(4,128)S(1)}, f32[16,512]{1,0:T(8,128)S(1)}, f32[512,512]{1,0:T(8,128)S(1)}, /*inde...) while((s32[]{:T(128)}, f32[128,512]{1,0:T(8,128)S(1)}, ...), condition=%wide.region_1.2_spmd.clone, body=%wide.region_0.1_spmd.clone.sunk | while | flops 403506688 | bytes 2372823 | solution.py:111
  124.4 7.9 %collective-permute-done.2 = f32[128,512]{1,0:T(8,128)S(1)} collective-permute-done((f32[128,512]{1,0:T(8,128)S(1)}, f32[128,512]{1,0:T(8,128)S(1)}, u32[]{:S(2)}, u32[]{:S(2)}) %collective-permute-start.2) | collective-permute-done | bytes 262176 | tf_op jit(solution)/shard_map/ppermute | solution.py:10
  134.3 7.9 %collective-permute-done.4 = f32[128,512]{1,0:T(8,128)S(1)} collective-permute-done((f32[128,512]{1,0:T(8,128)S(1)}, f32[128,512]{1,0:T(8,128)S(1)}, u32[]{:S(2)}, u32[]{:S(2)}) %collective-permute-start.4) | collective-permute-done | bytes 262176 | tf_op jit(solution)/shard_map/ppermute | solution.py:10
  142.9 24.7 %all-gather.15.cloned.1.call-done = f32[512,512]{1,0:T(8,128)} async-done(((f32[128,512]{1,0:T(8,128)}), f32[512,512]{1,0:T(8,128)}) %all-gather.15.cloned.1.call-update) | async-done | bytes 1048592 | tf_op jit(solution)/shard_map/all_gather | solution.py:88
  173.0 6.9 collective-permute-done.6
  187.3 19.8 %all-gather.17.cloned.1.call-done = f32[512,512]{1,0:T(8,128)} async-done(((f32[128,512]{1,0:T(8,128)}), f32[512,512]{1,0:T(8,128)}) %all-gather.17.cloned.1.call-update) | async-done | bytes 1048592 | tf_op jit(solution)/shard_map/all_gather | solution.py:88
  213.5 9.2 %collective-permute-done.8 = f32[128,512]{1,0:T(8,128)S(1)} collective-permute-done((f32[128,512]{1,0:T(8,128)S(1)}, f32[128,512]{1,0:T(8,128)S(1)}, u32[]{:S(2)}, u32[]{:S(2)}) %collective-permute-start.8) | collective-permute-done | bytes 262176 | tf_op jit(solution)/shard_map/ppermute | solution.py:10
  223.5 12.3 %all-gather.27.cloned.1.call-done = f32[512,512]{1,0:T(8,128)} async-done(((f32[128,512]{1,0:T(8,128)}), f32[512,512]{1,0:T(8,128)}) %all-gather.27.cloned.1.call-update) | async-done | bytes 1048592 | tf_op jit(solution)/shard_map/all_gather | solution.py:88
  237.7 5.2 collective-permute-start.20
  247.6 16.9 %all-gather.19.cloned.1.call-done = f32[512,512]{1,0:T(8,128)} async-done(((f32[128,512]{1,0:T(8,128)}), f32[512,512]{1,0:T(8,128)}) %all-gather.19.cloned.1.call-update) | async-done | bytes 1048592 | tf_op jit(solution)/shard_map/all_gather | solution.py:88
  266.4 7.6 collective-permute-start.10
  274.1 7.1 collective-permute-done.10
  282.0 11.2 %all-gather.29.cloned.1.call-done = f32[512,512]{1,0:T(8,128)} async-done(((f32[128,512]{1,0:T(8,128)}), f32[512,512]{1,0:T(8,128)}) %all-gather.29.cloned.1.call-update) | async-done | bytes 1048592 | tf_op jit(solution)/shard_map/all_gather | solution.py:88
  295.1 6.0 collective-permute-start.22
  301.2 9.1 %collective-permute-done.22 = f32[128,512]{1,0:T(8,128)S(1)} collective-permute-done((f32[128,512]{1,0:T(8,128)S(1)}, f32[128,512]{1,0:T(8,128)S(1)}, u32[]{:S(2)}, u32[]{:S(2)}) %collective-permute-start.22) | collective-permute-done | bytes 262176 | tf_op jit(solution)/shard_map/ppermute | solution.py:10
  311.1 11.0 %all-gather.21.cloned.1.call-done = f32[512,512]{1,0:T(8,128)} async-done(((f32[128,512]{1,0:T(8,128)}), f32[512,512]{1,0:T(8,128)}) %all-gather.21.cloned.1.call-update) | async-done | bytes 1048592 | tf_op jit(solution)/shard_map/all_gather | solution.py:88
  327.4 4.9 collective-permute-done.12
  333.1 17.9 %all-gather.31.cloned.1.call-done = f32[512,512]{1,0:T(8,128)} async-done(((f32[128,512]{1,0:T(8,128)}), f32[512,512]{1,0:T(8,128)}) %all-gather.31.cloned.1.call-update) | async-done | bytes 1048592 | tf_op jit(solution)/shard_map/all_gather | solution.py:88
  352.9 7.6 collective-permute-start.24
  360.5 9.2 %collective-permute-done.24 = f32[128,512]{1,0:T(8,128)} collective-permute-done((f32[128,512]{1,0:T(8,128)S(1)}, f32[128,512]{1,0:T(8,128)}, u32[]{:S(2)}, u32[]{:S(2)}) %collective-permute-start.24) | collective-permute-done | bytes 262176 | tf_op jit(solution)/shard_map/ppermute | solution.py:10
  369.8 10.0 %all-gather.23.cloned.1.call-done = f32[512,512]{1,0:T(8,128)} async-done(((f32[128,512]{1,0:T(8,128)}), f32[512,512]{1,0:T(8,128)}) %all-gather.23.cloned.1.call-update) | async-done | bytes 1048592 | tf_op jit(solution)/shard_map/all_gather | solution.py:88
  382.4 4.7 collective-permute-start.13
  396.1 5.1 collective-permute-done.1
  401.2 10.4 %all_gather.73 = f32[4,512]{1,0:T(4,128)S(1)} all-gather(f32[4,128]{1,0:T(4,128)S(1)} %collective-permute-done.1), channel_id=1, replica_groups=mesh['tm'=64,'state'=4] {'state'}, dimensions={1}, use_global_device_ids=true | all-gather | bytes 10240 | tf_op jit(solution)/shard_map/all_gather | solution.py:89
  413.8 5.7 collective-permute-done.3
  419.5 10.6 %all_gather.74 = f32[4,512]{1,0:T(4,128)S(1)} all-gather(f32[4,128]{1,0:T(4,128)S(1)} %collective-permute-done.3), channel_id=1, replica_groups=mesh['tm'=64,'state'=4] {'state'}, dimensions={1}, use_global_device_ids=true | all-gather | bytes 10240 | tf_op jit(solution)/shard_map/all_gather | solution.py:89
  432.3 6.6 collective-permute-done.5
  438.9 10.5 %all_gather.76 = f32[4,512]{1,0:T(4,128)S(1)} all-gather(f32[4,128]{1,0:T(4,128)S(1)} %collective-permute-done.5), channel_id=1, replica_groups=mesh['tm'=64,'state'=4] {'state'}, dimensions={1}, use_global_device_ids=true | all-gather | bytes 10240 | tf_op jit(solution)/shard_map/all_gather | solution.py:89
  453.8 6.2 collective-permute-done.7
  460.0 10.5 %all_gather.78 = f32[4,512]{1,0:T(4,128)S(1)} all-gather(f32[4,128]{1,0:T(4,128)S(1)} %collective-permute-done.7), channel_id=1, replica_groups=mesh['tm'=64,'state'=4] {'state'}, dimensions={1}, use_global_device_ids=true | all-gather | bytes 10240 | tf_op jit(solution)/shard_map/all_gather | solution.py:89
  476.2 10.7 %all_gather.80 = f32[4,512]{1,0:T(4,128)S(1)} all-gather(f32[4,128]{1,0:T(4,128)S(1)} %collective-permute-done.9), channel_id=1, replica_groups=mesh['tm'=64,'state'=4] {'state'}, dimensions={1}, use_global_device_ids=true | all-gather | bytes 10240 | tf_op jit(solution)/shard_map/all_gather | solution.py:89
  495.3 10.5 %all_gather.82 = f32[4,512]{1,0:T(4,128)S(1)} all-gather(f32[4,128]{1,0:T(4,128)S(1)} %collective-permute-done.11), channel_id=1, replica_groups=mesh['tm'=64,'state'=4] {'state'}, dimensions={1}, use_global_device_ids=true | all-gather | bytes 10240 | tf_op jit(solution)/shard_map/all_gather | solution.py:89
  513.4 4.5 all-to-all-done
  517.9 55.4 %while.70 = (s32[]{:T(128)}, f32[1,512]{1,0:T(1,128)S(1)}, f32[16,1,512]{2,1,0:T(1,128)S(1)}, f32[512,512]{1,0:T(8,128)S(1)}, f32[16,512]{1,0:T(8,128)S(1)}, /*i...) while((s32[]{:T(128)}, f32[1,512]{1,0:T(1,128)S(1)}, ...), condition=%wide.region_3.4_spmd, body=%wide.region_2.3_spmd.sunk | while | flops 3147267 | bytes 1063049 | solution.py:127
  574.9 30.2 %while.74 = (s32[]{:T(128)}, f32[1,512]{1,0:T(1,128)S(1)}, f32[16]{0:T(128)S(1)}, f32[512,512]{1,0:T(8,128)S(1)}, f32[16,512]{1,0:T(8,128)S(1)}, /*index=5*/f32[...) while((s32[]{:T(128)}, f32[1,512]{1,0:T(1,128)S(1)}, f32[16]{0:T(128)S(1)}, ...), condition=%wide.region_5.6_spmd.clone, body=%wide.region_4.5_spmd.clone.sunk | while | flops 3147780 | bytes 1065103 | solution.py:146
  605.1 7.6 all_to_all.48
  616.0 5.7 collective-permute-start.15
  623.0 10.4 %all_gather.85 = f32[4,512]{1,0:T(4,128)S(1)} all-gather(f32[4,128]{1,0:T(4,128)S(1)} %collective-permute-done.15), channel_id=1, replica_groups=mesh['tm'=64,'state'=4] {'state'}, dimensions={1}, use_global_device_ids=true | all-gather | bytes 10240 | tf_op jit(solution)/shard_map/all_gather | solution.py:89
  639.2 10.6 %all_gather.86 = f32[4,512]{1,0:T(4,128)S(1)} all-gather(f32[4,128]{1,0:T(4,128)S(1)} %collective-permute-done.17), channel_id=1, replica_groups=mesh['tm'=64,'state'=4] {'state'}, dimensions={1}, use_global_device_ids=true | all-gather | bytes 10240 | tf_op jit(solution)/shard_map/all_gather | solution.py:89
  656.5 10.4 %all_gather.88 = f32[4,512]{1,0:T(4,128)S(1)} all-gather(f32[4,128]{1,0:T(4,128)S(1)} %collective-permute-done.19), channel_id=1, replica_groups=mesh['tm'=64,'state'=4] {'state'}, dimensions={1}, use_global_device_ids=true | all-gather | bytes 10240 | tf_op jit(solution)/shard_map/all_gather | solution.py:89
  669.1 7.5 collective-permute-done.21
  676.6 10.6 %all_gather.90 = f32[4,512]{1,0:T(4,128)S(1)} all-gather(f32[4,128]{1,0:T(4,128)S(1)} %collective-permute-done.21), channel_id=1, replica_groups=mesh['tm'=64,'state'=4] {'state'}, dimensions={1}, use_global_device_ids=true | all-gather | bytes 10240 | tf_op jit(solution)/shard_map/all_gather | solution.py:89
  692.9 10.4 %all_gather.92 = f32[4,512]{1,0:T(4,128)S(1)} all-gather(f32[4,128]{1,0:T(4,128)S(1)} %collective-permute-done.23), channel_id=1, replica_groups=mesh['tm'=64,'state'=4] {'state'}, dimensions={1}, use_global_device_ids=true | all-gather | bytes 10240 | tf_op jit(solution)/shard_map/all_gather | solution.py:89
  710.7 10.6 %all_gather.94 = f32[4,512]{1,0:T(4,128)S(1)} all-gather(f32[4,128]{1,0:T(4,128)S(1)} %collective-permute-done.25), channel_id=1, replica_groups=mesh['tm'=64,'state'=4] {'state'}, dimensions={1}, use_global_device_ids=true | all-gather | bytes 10240 | tf_op jit(solution)/shard_map/all_gather | solution.py:89
  721.5 8.7 %all_to_all.49 = f32[4,1,128]{2,1,0:T(1,128)S(1)} all-to-all(f32[4,1,128]{2,1,0:T(1,128)S(1)} %bitcast.189), channel_id=1, replica_groups=mesh['tm'=64,'state'=4] {'state'}, dimensions={0} | all-to-all | bytes 4096 | tf_op jit(solution)/shard_map/all_to_all | solution.py:100
  730.2 30.3 %while.72 = (s32[]{:T(128)}, f32[1,512]{1,0:T(1,128)S(1)}, f32[16,1,512]{2,1,0:T(1,128)S(1)}, f32[16]{0:T(128)S(1)}, f32[512,512]{1,0:T(8,128)S(1)}, /*index=5*/...) while((s32[]{:T(128)}, f32[1,512]{1,0:T(1,128)S(1)}, f32[16,1,512]{2,1,0:T(1,128)S(1)}, ...), condition=%wide.region_9.10_spmd, body=%wide.region_8.9_spmd.sunk | while | flops 3147267 | bytes 1067141 | solution.py:159
  (516 shorter events, 321.0 us)
Async XLA Ops:
  7.2 500.6 %copy-start = (f32[4,512]{1,0:T(4,128)S(1)}, f32[4,512]{1,0:T(4,128)}, u32[]{:S(2)}) copy-start(f32[4,512]{1,0:T(4,128)} %param.18) | copy-start | bytes 24580
  7.2 32.2 %all-gather.13.cloned.1.call-start = ((), (), s32[]{:S(2)}) async-start(), calls=%async_computation.3 | async-start | bytes 1310720 | tf_op jit(solution)/shard_map/all_gather | solution.py:49
  7.9 159.7 %all-gather.15.cloned.1.call-start = ((), (), s32[]{:S(2)}) async-start(), calls=%async_computation.4 | async-start | bytes 1310720 | tf_op jit(solution)/shard_map/all_gather | solution.py:88
  39.3 1.2 copy-start.3
  81.1 43.2 %collective-permute-start.16 = (f32[128,512]{1,0:T(8,128)S(1)}, f32[128,512]{1,0:T(8,128)S(1)}, u32[]{:S(2)}, u32[]{:S(2)}) collective-permute-start(f32[128,512]{1,0:T(8,128)S(1)} %get-tuple-element.499), channel_id=1, source_target_pairs={{4,0},{8,4},{12,8},{16,12},{20,16},{24,20},{28,24},{32,28},{36,32}... | collective-permute-start | bytes 786440 | tf_op jit(solution)/shard_map/ppermute | solution.py:10
  122.4 9.8 %collective-permute-start.2 = (f32[128,512]{1,0:T(8,128)S(1)}, f32[128,512]{1,0:T(8,128)S(1)}, u32[]{:S(2)}, u32[]{:S(2)}) collective-permute-start(f32[128,512]{1,0:T(8,128)S(1)} %get-tuple-element.496), channel_id=1, source_target_pairs={{0,4},{4,8},{8,12},{12,16},{16,20},{20,24},{24,28},{28,32},{32,36}... | collective-permute-start | bytes 786440 | tf_op jit(solution)/shard_map/ppermute | solution.py:10
  132.3 9.8 %collective-permute-start.4 = (f32[128,512]{1,0:T(8,128)S(1)}, f32[128,512]{1,0:T(8,128)S(1)}, u32[]{:S(2)}, u32[]{:S(2)}) collective-permute-start(f32[128,512]{1,0:T(8,128)S(1)} %get-tuple-element.664), channel_id=1, source_target_pairs={{0,4},{4,8},{8,12},{12,16},{16,20},{20,24},{24,28},{28,32},{32,36}... | collective-permute-start | bytes 786440 | tf_op jit(solution)/shard_map/ppermute | solution.py:10
  142.9 64.2 %all-gather.17.cloned.1.call-start = ((), (), s32[]{:S(2)}) async-start(), calls=%async_computation.5 | async-start | bytes 1310720 | tf_op jit(solution)/shard_map/all_gather | solution.py:88
  169.5 10.4 %collective-permute-start.6 = (f32[128,512]{1,0:T(8,128)S(1)}, f32[128,512]{1,0:T(8,128)S(1)}, u32[]{:S(2)}, u32[]{:S(2)}) collective-permute-start(f32[128,512]{1,0:T(8,128)S(1)} %convolution_select_fusion.10), channel_id=1, source_target_pairs={{0,8},{4,12},{8,16},{12,20},{16,24},{20,28},{24,32},{28,36},{32,40... | collective-permute-start | bytes 786440 | tf_op jit(solution)/shard_map/ppermute | solution.py:10
  179.9 0.7 copy-start.12
  180.7 55.1 %all-gather.27.cloned.1.call-start = ((), (), s32[]{:S(2)}) async-start(), calls=%async_computation.10 | async-start | bytes 1310720 | tf_op jit(solution)/shard_map/all_gather | solution.py:88
  180.7 5.8 collective-permute-start.18
  186.5 0.7 copy-start.10
  187.2 77.2 %all-gather.19.cloned.1.call-start = ((), (), s32[]{:S(2)}) async-start(), calls=%async_computation.6 | async-start | bytes 1310720 | tf_op jit(solution)/shard_map/all_gather | solution.py:88
  209.0 13.7 %collective-permute-start.8 = (f32[128,512]{1,0:T(8,128)S(1)}, f32[128,512]{1,0:T(8,128)S(1)}, u32[]{:S(2)}, u32[]{:S(2)}) collective-permute-start(f32[128,512]{1,0:T(8,128)S(1)} %convolution_select_fusion.9), channel_id=1, source_target_pairs={{0,16},{4,20},{8,24},{12,28},{16,32},{20,36},{24,40},{28,44},{32,4... | collective-permute-start | bytes 786440 | tf_op jit(solution)/shard_map/ppermute | solution.py:10
  222.7 0.7 copy-start.11
  223.4 69.7 %all-gather.29.cloned.1.call-start = ((), (), s32[]{:S(2)}) async-start(), calls=%async_computation.11 | async-start | bytes 1310720 | tf_op jit(solution)/shard_map/all_gather | solution.py:88
  237.7 9.1 %collective-permute-start.20 = (f32[128,512]{1,0:T(8,128)S(1)}, f32[128,512]{1,0:T(8,128)S(1)}, u32[]{:S(2)}, u32[]{:S(2)}) collective-permute-start(f32[128,512]{1,0:T(8,128)S(1)} %convolution_select_fusion.4), channel_id=1, source_target_pairs={{8,0},{12,4},{16,8},{20,12},{24,16},{28,20},{32,24},{36,28},{40,32... | collective-permute-start | bytes 786440 | tf_op jit(solution)/shard_map/ppermute | solution.py:10
  247.5 74.5 %all-gather.21.cloned.1.call-start = ((), (), s32[]{:S(2)}) async-start(), calls=%async_computation.7 | async-start | bytes 1310720 | tf_op jit(solution)/shard_map/all_gather | solution.py:88
  266.4 14.8 %collective-permute-start.10 = (f32[128,512]{1,0:T(8,128)S(1)}, f32[128,512]{1,0:T(8,128)S(1)}, u32[]{:S(2)}, u32[]{:S(2)}) collective-permute-start(f32[128,512]{1,0:T(8,128)S(1)} %convolution_select_fusion.8), channel_id=1, source_target_pairs={{0,32},{4,36},{8,40},{12,44},{16,48},{20,52},{24,56},{28,60},{32,6... | collective-permute-start | bytes 786440 | tf_op jit(solution)/shard_map/ppermute | solution.py:10
  282.0 68.9 %all-gather.31.cloned.1.call-start = ((), (), s32[]{:S(2)}) async-start(), calls=%async_computation.12 | async-start | bytes 1310720 | tf_op jit(solution)/shard_map/all_gather | solution.py:88
  295.1 15.1 %collective-permute-start.22 = (f32[128,512]{1,0:T(8,128)S(1)}, f32[128,512]{1,0:T(8,128)S(1)}, u32[]{:S(2)}, u32[]{:S(2)}) collective-permute-start(f32[128,512]{1,0:T(8,128)S(1)} %convolution_select_fusion.3), channel_id=1, source_target_pairs={{16,0},{20,4},{24,8},{28,12},{32,16},{36,20},{40,24},{44,28},{48,3... | collective-permute-start | bytes 786440 | tf_op jit(solution)/shard_map/ppermute | solution.py:10
  311.0 68.8 %all-gather.23.cloned.1.call-start = ((), (), s32[]{:S(2)}) async-start(), calls=%async_computation.8 | async-start | bytes 1310720 | tf_op jit(solution)/shard_map/all_gather | solution.py:88
  324.0 8.3 %collective-permute-start.12 = (f32[128,512]{1,0:T(8,128)S(1)}, f32[128,512]{1,0:T(8,128)S(1)}, u32[]{:S(2)}, u32[]{:S(2)}) collective-permute-start(f32[128,512]{1,0:T(8,128)S(1)} %convolution_select_fusion.7), channel_id=1, source_target_pairs={{0,64},{4,68},{8,72},{12,76},{16,80},{20,84},{24,88},{28,92},{32,9... | collective-permute-start | bytes 786440 | tf_op jit(solution)/shard_map/ppermute | solution.py:10
  333.0 156.7 %all-gather.33.cloned.1.call-start = ((), (), s32[]{:S(2)}) async-start(), calls=%async_computation.13 | async-start | bytes 1310720 | tf_op jit(solution)/shard_map/all_gather | solution.py:88
  352.9 16.8 %collective-permute-start.24 = (f32[128,512]{1,0:T(8,128)S(1)}, f32[128,512]{1,0:T(8,128)}, u32[]{:S(2)}, u32[]{:S(2)}) collective-permute-start(f32[128,512]{1,0:T(8,128)S(1)} %convolution_select_fusion.2), channel_id=1, source_target_pairs={{32,0},{36,4},{40,8},{44,12},{48,16},{52,20},{56,24},{60,28},{64,3... | collective-permute-start | bytes 786440 | tf_op jit(solution)/shard_map/ppermute | solution.py:10
  369.7 136.1 %all-gather.25.cloned.1.call-start = ((), (), s32[]{:S(2)}) async-start(), calls=%async_computation.9 | async-start | bytes 1310720 | tf_op jit(solution)/shard_map/all_gather | solution.py:88
  381.7 0.7 copy-start.1
  382.4 7.9 %collective-permute-start.13 = (f32[128,512]{1,0:T(8,128)S(1)}, f32[128,512]{1,0:T(8,128)}, u32[]{:S(2)}, u32[]{:S(2)}) collective-permute-start(f32[128,512]{1,0:T(8,128)S(1)} %convolution_select_fusion.6), channel_id=1, source_target_pairs={{0,128},{4,132},{8,136},{12,140},{16,144},{20,148},{24,152},{28,15... | collective-permute-start | bytes 786440 | tf_op jit(solution)/shard_map/ppermute | solution.py:10
  387.1 7.0 collective-permute-start
  394.1 7.0 collective-permute-start.1
  411.8 7.7 collective-permute-start.3
  430.3 8.6 %collective-permute-start.5 = (f32[4,128]{1,0:T(4,128)S(1)}, f32[4,128]{1,0:T(4,128)S(1)}, u32[]{:S(2)}, u32[]{:S(2)}) collective-permute-start(f32[4,128]{1,0:T(4,128)S(1)} %fusion.33), channel_id=1, source_target_pairs={{0,16},{4,20},{8,24},{12,28},{16,32},{20,36},{24,40},{28,44},{32,4... | collective-permute-start | bytes 6152 | tf_op jit(solution)/shard_map/ppermute | solution.py:10
  449.6 10.4 %collective-permute-start.7 = (f32[4,128]{1,0:T(4,128)S(1)}, f32[4,128]{1,0:T(4,128)S(1)}, u32[]{:S(2)}, u32[]{:S(2)}) collective-permute-start(f32[4,128]{1,0:T(4,128)S(1)} %fusion.32), channel_id=1, source_target_pairs={{0,32},{4,36},{8,40},{12,44},{16,48},{20,52},{24,56},{28,60},{32,6... | collective-permute-start | bytes 6152 | tf_op jit(solution)/shard_map/ppermute | solution.py:10
  470.7 5.5 collective-permute-start.9
  487.2 18.6 %copy-start.2 = (f32[128,512]{1,0:T(8,128)S(1)}, f32[128,512]{1,0:T(8,128)}, u32[]{:S(2)}) copy-start(f32[128,512]{1,0:T(8,128)} %copy-done.1) | copy-start | bytes 786436
  487.2 8.1 %collective-permute-start.11 = (f32[4,128]{1,0:T(4,128)S(1)}, f32[4,128]{1,0:T(4,128)S(1)}, u32[]{:S(2)}, u32[]{:S(2)}) collective-permute-start(f32[4,128]{1,0:T(4,128)S(1)} %fusion.30), channel_id=1, source_target_pairs={{0,128},{4,132},{8,136},{12,140},{16,144},{20,148},{24,152},{28,15... | collective-permute-start | bytes 6152 | tf_op jit(solution)/shard_map/ppermute | solution.py:10
  491.7 21.0 %collective-permute-start.26 = (f32[128,512]{1,0:T(8,128)S(1)}, f32[128,512]{1,0:T(8,128)S(1)}, u32[]{:S(2)}, u32[]{:S(2)}) collective-permute-start(f32[128,512]{1,0:T(8,128)S(1)} %convolution_select_fusion.1), channel_id=1, source_target_pairs={{64,0},{68,4},{72,8},{76,12},{80,16},{84,20},{88,24},{92,28},{96,3... | collective-permute-start | bytes 786440 | tf_op jit(solution)/shard_map/ppermute | solution.py:10
  509.0 8.9 %all-to-all-start = ((f32[4,1,128]{2,1,0:T(1,128)}), f32[4,1,128]{2,1,0:T(1,128)S(1)}, u32[]{:S(2)}, u32[]{:S(2)}) async-start(f32[4,1,128]{2,1,0:T(1,128)} %bitcast.18), calls=%async_computation | async-start | bytes 4096 | tf_op jit(solution)/shard_map/all_to_all | solution.py:100
  512.6 192.4 %all-gather.35.cloned.1.call-start = ((), (), s32[]{:S(2)}) async-start(), calls=%async_computation.14 | async-start | bytes 1310720 | tf_op jit(solution)/shard_map/all_gather | solution.py:88
  573.2 1.0 copy-start.4
  612.8 3.2 collective-permute-start.14
  616.0 7.0 collective-permute-start.15
  633.6 5.5 collective-permute-start.17
  650.0 6.4 collective-permute-start.19
  667.1 9.5 %collective-permute-start.21 = (f32[4,128]{1,0:T(4,128)S(1)}, f32[4,128]{1,0:T(4,128)S(1)}, u32[]{:S(2)}, u32[]{:S(2)}) collective-permute-start(f32[4,128]{1,0:T(4,128)S(1)} %fusion.25), channel_id=1, source_target_pairs={{32,0},{36,4},{40,8},{44,12},{48,16},{52,20},{56,24},{60,28},{64,3... | collective-permute-start | bytes 6152 | tf_op jit(solution)/shard_map/ppermute | solution.py:10
  687.4 5.5 collective-permute-start.23
  703.6 7.1 collective-permute-start.25
  (11 other events, 7.5 us)
Sparse Core Ops, SparseCore 0:
  9.8 29.4 all-gather.12
  143.0 24.5 all-gather.14
  180.8 26.2 all-gather.16
  208.7 27.0 all-gather.26
  237.4 27.0 all-gather.18
  266.1 27.0 all-gather.28
  295.0 27.0 all-gather.20
  323.9 27.0 all-gather.30
  352.7 27.0 all-gather.22
  381.4 27.0 all-gather.32
  410.3 27.0 all-gather.24
  514.9 23.5 all-gather.34
where the time goes:
time: 770 us; the launch traced here: 768 us
  waiting for transfers between devices  285 us (37%)
  blocking collectives  142 us (18%)
  matrix products  117 us (15%)
  starting transfers between devices  91.9 us (12%)
  local copies, waits for them, and re-layouts  61 us (8%)
  other arithmetic  53.3 us (7%)
  between operations  14.8 us (2%)
    ppermute x27, waiting for transfers between devices, passed_along(): return lax.ppermute(block, axis, route)  127 us
    all_gather x12, blocking collectives, doubling(): lax.all_gather(arrived[1], 'state', axis=1, tiled=True)  126 us
    all_gather x11, waiting for transfers between devices, doubling(): lax.all_gather(arrived[0], 'state', axis=0, tiled=True)  124 us
    ppermute x27, starting transfers between devices, passed_along(): return lax.ppermute(block, axis, route)  87.8 us
    dot_general x46, matrix products, transposed(): lax.dot_general(left, right, (((1,), (1,)), ((), ())), precision=lax.Prec...  59.6 us
    dot_general x76, matrix products, product(): jnp.dot(left, right, precision=lax.Precision.HIGHEST, preferred_element_t...  57.1 us
    dynamic_slice x112, local copies, waits for them, and re-layouts, per_device(): lax.scan(filter_portion, (owned_rows, initial_shifts), (observed_masks, s...  49.2 us
    all_gather x1, waiting for transfers between devices, per_device(): lax.all_gather(dynamics, 'state', axis=0, tiled=True) * block_mask  29 us
  transfers between devices with their start and end apart: 40, of which 34 were waited for; matrix products, arithmetic and copies ran while one was open for 19% of the time, Pallas kernels for 0%

commit v1 on v0

--- a/solution.py
+++ b/solution.py
@@ -1,7 +1,39 @@
+import functools
 import jax
 import jax.numpy as jnp
 from jax import lax
 from jax.sharding import PartitionSpec as P
+
+
+def roots_handle(sample, join_dim):
+    piece_now, fresh, tile_out = (
+        lax.psum(1, "state"),
+        lax.axis_index("state"),
+        sample.shape[join_dim],
+    )
+    sides = tuple(((to_i, (to_i + 1) % piece_now) for to_i in range(piece_now)))
+    all_blocks = tuple(((to_i, (to_i - 1) % piece_now) for to_i in range(piece_now)))
+    all_rows = jnp.zeros(
+        (*sample.shape[:join_dim], piece_now * tile_out, *sample.shape[join_dim + 1 :]),
+        sample.dtype,
+    )
+    all_rows = lax.dynamic_update_slice_in_dim(all_rows, sample, fresh * tile_out, axis=join_dim)
+    built = carry_in = sample
+    part_next = piece_now // 2
+    for s in range(1, part_next + 1):
+        built = lax.ppermute(built, "state", sides)
+        all_rows = lax.dynamic_update_slice_in_dim(
+            all_rows, built, (fresh - s) % piece_now * tile_out, axis=join_dim
+        )
+        if s < piece_now - part_next:
+            carry_in = lax.ppermute(carry_in, "state", perm=all_blocks)
+            all_rows = lax.dynamic_update_slice_in_dim(
+                all_rows, carry_in, (fresh + s) % piece_now * tile_out, axis=join_dim
+            )
+    return all_rows
+
+
+register_orders_in = functools.partial(roots_handle, join_dim=0)
 
 
 def passed_along(block, axis, distance):
@@ -85,7 +117,7 @@
                 current = select_tree(usable, arrived, identity)
             else:
                 gathered = (
-                    lax.all_gather(arrived[0], "state", axis=0, tiled=True),
+                    register_orders_in(arrived[0]),
                     lax.all_gather(arrived[1], "state", axis=1, tiled=True),
                 )
                 current = select_tree(usable, combine_rows(gathered, current), current)

time: 770 us -> 667 us (0.87); the launches traced: 768 us -> 656 us
  waiting for transfers between devices: 285 us -> 151 us
  starting transfers between devices: 91.9 us -> 129 us
  matrix products: 117 us -> 103 us
    all_gather x11 -> x0, waiting for transfers between devices: 124 us -> none  [doubling(): lax.all_gather(arrived[0], 'state', axis=0, tiled=True)]
    ppermute x27, waiting for transfers between devices: 127 us -> 64.6 us  [passed_along(): return lax.ppermute(block, axis, route)]
    ppermute x0 -> x33, waiting for transfers between devices: none -> 55.9 us  [the longest x22 55.9 us: roots_handle(): built = lax.ppermute(built, 'state', sides)]
    ppermute x0 -> x33, starting transfers between devices: none -> 39.4 us  [the longest x11 20.3 us: roots_handle(): carry_in = lax.ppermute(carry_in, 'state', perm=all_blocks)]
    dot_general x76, matrix products: 57.1 us -> 43.6 us  [product(): jnp.dot(left, right, precision=lax.Precision.HIGHEST, preferred_element_t...]
  transfers between devices with their start and end apart: 40 -> 62, of which waited for: 34 -> 31; matrix products, arithmetic and copies ran while one was open for 19% -> 21% of each run, Pallas kernels for 0% -> 0%
where the time goes in v1:
time: 667 us; the launch traced here: 656 us
  waiting for transfers between devices  151 us (23%)
  blocking collectives  145 us (22%)
  starting transfers between devices  129 us (19%)
  matrix products  103 us (15%)
  local copies, waits for them, and re-layouts  57.3 us (9%)
  other arithmetic  53.3 us (8%)
  between operations  15.4 us (2%)
    all_gather x12, blocking collectives, doubling(): lax.all_gather(arrived[1], 'state', axis=1, tiled=True)  126 us
    ppermute x27, starting transfers between devices, passed_along(): return lax.ppermute(block, axis, route)  86.1 us
    ppermute x27, waiting for transfers between devices, passed_along(): return lax.ppermute(block, axis, route)  64.6 us
    dot_general x46, matrix products, transposed(): lax.dot_general(left, right, (((1,), (1,)), ((), ())), precision=lax.Prec...  59.6 us
    ppermute x22, waiting for transfers between devices, roots_handle(): built = lax.ppermute(built, 'state', sides)  55.9 us
    dynamic_slice x112, local copies, waits for them, and re-layouts, per_device(): lax.scan(filter_portion, (owned_rows, initial_shifts), (observed_masks, s...  48.4 us
    dot_general x76, matrix products, product(): jnp.dot(left, right, precision=lax.Precision.HIGHEST, preferred_element_t...  43.6 us
    all_gather x1, waiting for transfers between devices, per_device(): lax.all_gather(dynamics, 'state', axis=0, tiled=True) * block_mask  29 us
  transfers between devices with their start and end apart: 62, of which 31 were waited for; matrix products, arithmetic and copies ran while one was open for 21% of the time, Pallas kernels for 0%

profile of v1, /device:TPU:8, one launch (start us, length us, event | category | flops | bytes accessed | tf_op | source)
XLA Modules:
  0.0 656.1 jit_solution(11681607745434436850)
XLA Ops:
  10.3 29.0 %all-gather.2.cloned.1.call-done = f32[512,512]{1,0:T(8,128)} async-done(((f32[128,512]{1,0:T(8,128)}), f32[512,512]{1,0:T(8,128)}) %all-gather.2.cloned.1.call-update) | async-done | bytes 1048592 | tf_op jit(solution)/shard_map/all_gather | solution.py:81
  40.8 39.6 %while.71 = (s32[]{:T(128)}, f32[128,512]{1,0:T(8,128)S(1)}, f32[16]{0:T(128)S(1)}, f32[16,512]{1,0:T(8,128)S(1)}, f32[512,512]{1,0:T(8,128)S(1)}, /*index=5*/s32[]{:T(128)}) while((s32[]{:T(128)}, f32[128,512]{1,0:T(8,128)S(1)}, f32[16]{0:T(128)S(1)}, f32[16,512]{1,0:T(8,128)S(1)}, f32[512,512]{1,0:T(8,128)S(1)}, /*index=5*/s32[]{:T(128)}) %tuple.143), condition=%wide.region_7.8_spmd, body=%wide.region_6.7_spmd.sunk | while | flops 402784256 | bytes 2103393 | solution.py:187
  83.0 38.8 %while.73 = (s32[]{:T(128)}, f32[128,512]{1,0:T(8,128)S(1)}, f32[4,128]{1,0:T(4,128)S(1)}, f32[16,512]{1,0:T(8,128)S(1)}, f32[512,512]{1,0:T(8,128)S(1)}, /*inde...) while((s32[]{:T(128)}, f32[128,512]{1,0:T(8,128)S(1)}, ...), condition=%wide.region_1.2_spmd.clone, body=%wide.region_0.1_spmd.clone.sunk | while | flops 403506688 | bytes 2372823 | solution.py:143
  123.7 7.9 %collective-permute-done.2 = f32[128,512]{1,0:T(8,128)S(1)} collective-permute-done((f32[128,512]{1,0:T(8,128)S(1)}, f32[128,512]{1,0:T(8,128)S(1)}, u32[]{:S(2)}, u32[]{:S(2)}) %collective-permute-start.2) | collective-permute-done | bytes 262176 | tf_op jit(solution)/shard_map/ppermute | solution.py:42
  133.6 5.8 collective-permute-start.36
  147.5 4.3 collective-permute-done.5
  151.8 5.6 collective-permute-done.37
  157.6 3.5 collective-permute-done.7
  165.8 4.8 collective-permute-start.41
  172.6 5.0 collective-permute-done
  179.6 5.1 collective-permute-done.1
  184.6 10.4 %all_gather.40 = f32[4,512]{1,0:T(4,128)S(1)} all-gather(f32[4,128]{1,0:T(4,128)S(1)} %collective-permute-done.1), channel_id=1, replica_groups=mesh['tm'=64,'state'=4] {'state'}, dimensions={1}, use_global_device_ids=true | all-gather | bytes 10240 | tf_op jit(solution)/shard_map/all_gather | solution.py:121
  200.0 5.2 collective-permute-done.42
  213.6 4.9 collective-permute-start.46
  218.4 3.7 collective-permute-done.14
  225.1 5.7 collective-permute-done.3
  230.8 10.9 %all_gather.41 = f32[4,512]{1,0:T(4,128)S(1)} all-gather(f32[4,128]{1,0:T(4,128)S(1)} %collective-permute-done.3), channel_id=1, replica_groups=mesh['tm'=64,'state'=4] {'state'}, dimensions={1}, use_global_device_ids=true | all-gather | bytes 10240 | tf_op jit(solution)/shard_map/all_gather | solution.py:121
  245.7 6.6 collective-permute-done.8
  252.3 10.4 %all_gather.42 = f32[4,512]{1,0:T(4,128)S(1)} all-gather(f32[4,128]{1,0:T(4,128)S(1)} %collective-permute-done.8), channel_id=1, replica_groups=mesh['tm'=64,'state'=4] {'state'}, dimensions={1}, use_global_device_ids=true | all-gather | bytes 10240 | tf_op jit(solution)/shard_map/all_gather | solution.py:121
  267.2 6.6 %collective-permute-done.17 = f32[128,512]{1,0:T(8,128)S(1)} collective-permute-done((f32[128,512]{1,0:T(8,128)}, f32[128,512]{1,0:T(8,128)S(1)}, u32[]{:S(2)}, u32[]{:S(2)}) %collective-permute-start.17) | collective-permute-done | bytes 262176 | tf_op jit(solution)/shard_map/ppermute | solution.py:24
  276.9 8.6 %collective-permute-start.13 = (f32[4,128]{1,0:T(4,128)S(1)}, f32[4,128]{1,0:T(4,128)S(1)}, u32[]{:S(2)}, u32[]{:S(2)}) collective-permute-start(f32[4,128]{1,0:T(4,128)S(1)} %fusion.32), channel_id=1, source_target_pairs={{0,32},{4,36},{8,40},{12,44},{16,48},{20,52},{24,56},{28,60},{32,6... | collective-permute-start | bytes 6152 | tf_op jit(solution)/shard_map/ppermute | solution.py:42
  285.6 4.5 collective-permute-done.13
  290.0 10.4 %all_gather.43 = f32[4,512]{1,0:T(4,128)S(1)} all-gather(f32[4,128]{1,0:T(4,128)S(1)} %collective-permute-done.13), channel_id=1, replica_groups=mesh['tm'=64,'state'=4] {'state'}, dimensions={1}, use_global_device_ids=true | all-gather | bytes 10240 | tf_op jit(solution)/shard_map/all_gather | solution.py:121
  304.3 3.7 collective-permute-done.49
  311.6 6.8 %collective-permute-done.22 = f32[128,512]{1,0:T(8,128)S(1)} collective-permute-done((f32[128,512]{1,0:T(8,128)S(1)}, f32[128,512]{1,0:T(8,128)S(1)}, u32[]{:S(2)}, u32[]{:S(2)}) %collective-permute-start.22) | collective-permute-done | bytes 262176 | tf_op jit(solution)/shard_map/ppermute | solution.py:24
  323.3 5.0 collective-permute-start.51
  335.1 10.6 %all_gather.44 = f32[4,512]{1,0:T(4,128)S(1)} all-gather(f32[4,128]{1,0:T(4,128)S(1)} %collective-permute-done.18), channel_id=1, replica_groups=mesh['tm'=64,'state'=4] {'state'}, dimensions={1}, use_global_device_ids=true | all-gather | bytes 10240 | tf_op jit(solution)/shard_map/all_gather | solution.py:121
  350.2 6.2 collective-permute-done.27
  364.0 6.0 collective-permute-start.23
  372.7 10.5 %all_gather.45 = f32[4,512]{1,0:T(4,128)S(1)} all-gather(f32[4,128]{1,0:T(4,128)S(1)} %collective-permute-done.23), channel_id=1, replica_groups=mesh['tm'=64,'state'=4] {'state'}, dimensions={1}, use_global_device_ids=true | all-gather | bytes 10240 | tf_op jit(solution)/shard_map/all_gather | solution.py:121
  386.1 5.0 collective-permute-done.31
  397.0 4.1 collective-permute-start.56
  401.5 55.4 %while.70 = (s32[]{:T(128)}, f32[1,512]{1,0:T(1,128)S(1)}, f32[16,1,512]{2,1,0:T(1,128)S(1)}, f32[512,512]{1,0:T(8,128)S(1)}, f32[16,512]{1,0:T(8,128)S(1)}, /*i...) while((s32[]{:T(128)}, f32[1,512]{1,0:T(1,128)S(1)}, ...), condition=%wide.region_3.4_spmd, body=%wide.region_2.3_spmd.sunk | while | flops 3147267 | bytes 1063049 | solution.py:159
  458.5 30.2 %while.74 = (s32[]{:T(128)}, f32[1,512]{1,0:T(1,128)S(1)}, f32[16]{0:T(128)S(1)}, f32[512,512]{1,0:T(8,128)S(1)}, f32[16,512]{1,0:T(8,128)S(1)}, /*index=5*/f32[...) while((s32[]{:T(128)}, f32[1,512]{1,0:T(1,128)S(1)}, f32[16]{0:T(128)S(1)}, ...), condition=%wide.region_5.6_spmd.clone, body=%wide.region_4.5_spmd.clone.sunk | while | flops 3147780 | bytes 1065103 | solution.py:178
  488.8 9.6 %all_to_all.48 = f32[1,4,128]{2,0,1:T(1,128)S(1)} all-to-all(f32[1,4,128]{2,0,1:T(1,128)S(1)} %bitcast.186), channel_id=1, replica_groups=mesh['tm'=64,'state'=4] {'state'}, dimensions={1} | all-to-all | bytes 4096 | tf_op jit(solution)/shard_map/all_to_all | solution.py:181
  501.5 5.7 collective-permute-start.33
  510.6 10.6 %all_gather.46 = f32[4,512]{1,0:T(4,128)S(1)} all-gather(f32[4,128]{1,0:T(4,128)S(1)} %collective-permute-done.33), channel_id=1, replica_groups=mesh['tm'=64,'state'=4] {'state'}, dimensions={1}, use_global_device_ids=true | all-gather | bytes 10240 | tf_op jit(solution)/shard_map/all_gather | solution.py:121
  526.9 10.6 %all_gather.47 = f32[4,512]{1,0:T(4,128)S(1)} all-gather(f32[4,128]{1,0:T(4,128)S(1)} %collective-permute-done.35), channel_id=1, replica_groups=mesh['tm'=64,'state'=4] {'state'}, dimensions={1}, use_global_device_ids=true | all-gather | bytes 10240 | tf_op jit(solution)/shard_map/all_gather | solution.py:121
  539.8 4.4 collective-permute-done.40
  544.3 10.6 %all_gather.48 = f32[4,512]{1,0:T(4,128)S(1)} all-gather(f32[4,128]{1,0:T(4,128)S(1)} %collective-permute-done.40), channel_id=1, replica_groups=mesh['tm'=64,'state'=4] {'state'}, dimensions={1}, use_global_device_ids=true | all-gather | bytes 10240 | tf_op jit(solution)/shard_map/all_gather | solution.py:121
  558.4 6.1 collective-permute-done.45
  564.5 10.4 %all_gather.49 = f32[4,512]{1,0:T(4,128)S(1)} all-gather(f32[4,128]{1,0:T(4,128)S(1)} %collective-permute-done.45), channel_id=1, replica_groups=mesh['tm'=64,'state'=4] {'state'}, dimensions={1}, use_global_device_ids=true | all-gather | bytes 10240 | tf_op jit(solution)/shard_map/all_gather | solution.py:121
  577.2 3.5 collective-permute-done.50
  580.7 10.6 %all_gather.50 = f32[4,512]{1,0:T(4,128)S(1)} all-gather(f32[4,128]{1,0:T(4,128)S(1)} %collective-permute-done.50), channel_id=1, replica_groups=mesh['tm'=64,'state'=4] {'state'}, dimensions={1}, use_global_device_ids=true | all-gather | bytes 10240 | tf_op jit(solution)/shard_map/all_gather | solution.py:121
  593.6 5.0 collective-permute-done.55
  598.6 10.4 %all_gather.51 = f32[4,512]{1,0:T(4,128)S(1)} all-gather(f32[4,128]{1,0:T(4,128)S(1)} %collective-permute-done.55), channel_id=1, replica_groups=mesh['tm'=64,'state'=4] {'state'}, dimensions={1}, use_global_device_ids=true | all-gather | bytes 10240 | tf_op jit(solution)/shard_map/all_gather | solution.py:121
  609.3 8.9 %all_to_all.49 = f32[4,1,128]{2,1,0:T(1,128)S(1)} all-to-all(f32[4,1,128]{2,1,0:T(1,128)S(1)} %bitcast.189), channel_id=1, replica_groups=mesh['tm'=64,'state'=4] {'state'}, dimensions={0} | all-to-all | bytes 4096 | tf_op jit(solution)/shard_map/all_to_all | solution.py:132
  618.1 30.3 %while.72 = (s32[]{:T(128)}, f32[1,512]{1,0:T(1,128)S(1)}, f32[16,1,512]{2,1,0:T(1,128)S(1)}, f32[16]{0:T(128)S(1)}, f32[512,512]{1,0:T(8,128)S(1)}, /*index=5*/...) while((s32[]{:T(128)}, f32[1,512]{1,0:T(1,128)S(1)}, f32[16,1,512]{2,1,0:T(1,128)S(1)}, ...), condition=%wide.region_9.10_spmd, body=%wide.region_8.9_spmd.sunk | while | flops 3147267 | bytes 1067141 | solution.py:191
  (582 shorter events, 315.0 us)
Async XLA Ops:
  7.2 32.2 %all-gather.2.cloned.1.call-start = ((), (), s32[]{:S(2)}) async-start(), calls=%async_computation.3 | async-start | bytes 1310720 | tf_op jit(solution)/shard_map/all_gather | solution.py:81
  80.4 43.3 %collective-permute-start.34 = (f32[128,512]{1,0:T(8,128)S(1)}, f32[128,512]{1,0:T(8,128)S(1)}, u32[]{:S(2)}, u32[]{:S(2)}) collective-permute-start(f32[128,512]{1,0:T(8,128)S(1)} %get-tuple-element.499), channel_id=1, source_target_pairs={{4,0},{8,4},{12,8},{16,12},{20,16},{24,20},{28,24},{32,28},{36,32}... | collective-permute-start | bytes 786440 | tf_op jit(solution)/shard_map/ppermute | solution.py:42
  121.7 9.8 %collective-permute-start.2 = (f32[128,512]{1,0:T(8,128)S(1)}, f32[128,512]{1,0:T(8,128)S(1)}, u32[]{:S(2)}, u32[]{:S(2)}) collective-permute-start(f32[128,512]{1,0:T(8,128)S(1)} %get-tuple-element.496), channel_id=1, source_target_pairs={{0,4},{4,8},{8,12},{12,16},{16,20},{20,24},{24,28},{28,32},{32,36}... | collective-permute-start | bytes 786440 | tf_op jit(solution)/shard_map/ppermute | solution.py:42
  131.6 9.8 %collective-permute-start.4 = (f32[128,512]{1,0:T(8,128)S(1)}, f32[128,512]{1,0:T(8,128)S(1)}, u32[]{:S(2)}, u32[]{:S(2)}) collective-permute-start(f32[128,512]{1,0:T(8,128)S(1)} %get-tuple-element.664), channel_id=1, source_target_pairs={{0,4},{4,8},{8,12},{12,16},{16,20},{20,24},{24,28},{28,32},{32,36}... | collective-permute-start | bytes 786440 | tf_op jit(solution)/shard_map/ppermute | solution.py:42
  133.6 9.6 %collective-permute-start.36 = (f32[128,512]{1,0:T(8,128)S(1)}, f32[128,512]{1,0:T(8,128)S(1)}, u32[]{:S(2)}, u32[]{:S(2)}) collective-permute-start(f32[128,512]{1,0:T(8,128)S(1)} %get-tuple-element.663), channel_id=1, source_target_pairs={{4,0},{8,4},{12,8},{16,12},{20,16},{24,20},{28,24},{32,28},{36,32}... | collective-permute-start | bytes 786440 | tf_op jit(solution)/shard_map/ppermute | solution.py:42
  141.4 10.4 %collective-permute-start.5 = (f32[128,512]{1,0:T(8,128)S(1)}, f32[128,512]{1,0:T(8,128)S(1)}, u32[]{:S(2)}, u32[]{:S(2)}) collective-permute-start(f32[128,512]{1,0:T(8,128)S(1)} %collective-permute-done.4), channel_id=1, source_target_pairs={{0,1},{1,2},{2,3},{3,0},{4,5},{5,6},{6,7},{7,4},{8,9},{9,10},{10,1... | collective-permute-start | bytes 786440 | tf_op jit(solution)/shard_map/ppermute | solution.py:24
  143.2 14.3 %collective-permute-start.37 = (f32[128,512]{1,0:T(8,128)S(1)}, f32[128,512]{1,0:T(8,128)S(1)}, u32[]{:S(2)}, u32[]{:S(2)}) collective-permute-start(f32[128,512]{1,0:T(8,128)S(1)} %collective-permute-done.36), channel_id=1, source_target_pairs={{0,1},{1,2},{2,3},{3,0},{4,5},{5,6},{6,7},{7,4},{8,9},{9,10},{10,1... | collective-permute-start | bytes 786440 | tf_op jit(solution)/shard_map/ppermute | solution.py:24
  144.0 13.5 %collective-permute-start.6 = (f32[128,512]{1,0:T(8,128)S(1)}, f32[128,512]{1,0:T(8,128)S(1)}, u32[]{:S(2)}, u32[]{:S(2)}) collective-permute-start(f32[128,512]{1,0:T(8,128)S(1)} %collective-permute-done.4), channel_id=1, source_target_pairs={{0,3},{1,0},{2,1},{3,2},{4,7},{5,4},{6,5},{7,6},{8,11},{9,8},{10,9... | collective-permute-start | bytes 786440 | tf_op jit(solution)/shard_map/ppermute | solution.py:29
  146.4 11.1 %collective-permute-start.38 = (f32[128,512]{1,0:T(8,128)S(1)}, f32[128,512]{1,0:T(8,128)S(1)}, u32[]{:S(2)}, u32[]{:S(2)}) collective-permute-start(f32[128,512]{1,0:T(8,128)S(1)} %collective-permute-done.36), channel_id=1, source_target_pairs={{0,3},{1,0},{2,1},{3,2},{4,7},{5,4},{6,5},{7,6},{8,11},{9,8},{10,9... | collective-permute-start | bytes 786440 | tf_op jit(solution)/shard_map/ppermute | solution.py:29
  151.8 9.3 %collective-permute-start.7 = (f32[128,512]{1,0:T(8,128)S(1)}, f32[128,512]{1,0:T(8,128)S(1)}, u32[]{:S(2)}, u32[]{:S(2)}) collective-permute-start(f32[128,512]{1,0:T(8,128)S(1)} %collective-permute-done.5), channel_id=1, source_target_pairs={{0,1},{1,2},{2,3},{3,0},{4,5},{5,6},{6,7},{7,4},{8,9},{9,10},{10,1... | collective-permute-start | bytes 786440 | tf_op jit(solution)/shard_map/ppermute | solution.py:24
  161.9 10.7 %collective-permute-start.9 = (f32[128,512]{1,0:T(8,128)S(1)}, f32[128,512]{1,0:T(8,128)S(1)}, u32[]{:S(2)}, u32[]{:S(2)}) collective-permute-start(f32[128,512]{1,0:T(8,128)S(1)} %convolution_select_fusion.10), channel_id=1, source_target_pairs={{0,8},{4,12},{8,16},{12,20},{16,24},{20,28},{24,32},{28,36},{32,40... | collective-permute-start | bytes 786440 | tf_op jit(solution)/shard_map/ppermute | solution.py:42
  165.8 29.4 %collective-permute-start.41 = (f32[128,512]{1,0:T(8,128)S(1)}, f32[128,512]{1,0:T(8,128)S(1)}, u32[]{:S(2)}, u32[]{:S(2)}) collective-permute-start(f32[128,512]{1,0:T(8,128)S(1)} %convolution_select_fusion.4), channel_id=1, source_target_pairs={{8,0},{12,4},{16,8},{20,12},{24,16},{28,20},{32,24},{36,28},{40,32... | collective-permute-start | bytes 786440 | tf_op jit(solution)/shard_map/ppermute | solution.py:42
  172.5 26.6 %collective-permute-start.10 = (f32[128,512]{1,0:T(8,128)S(1)}, f32[128,512]{1,0:T(8,128)S(1)}, u32[]{:S(2)}, u32[]{:S(2)}) collective-permute-start(f32[128,512]{1,0:T(8,128)S(1)} %collective-permute-done.9), channel_id=1, source_target_pairs={{0,1},{1,2},{2,3},{3,0},{4,5},{5,6},{6,7},{7,4},{8,9},{9,10},{10,1... | collective-permute-start | bytes 786440 | tf_op jit(solution)/shard_map/ppermute | solution.py:24
  195.1 10.2 %collective-permute-start.11 = (f32[128,512]{1,0:T(8,128)S(1)}, f32[128,512]{1,0:T(8,128)S(1)}, u32[]{:S(2)}, u32[]{:S(2)}) collective-permute-start(f32[128,512]{1,0:T(8,128)S(1)} %collective-permute-done.9), channel_id=1, source_target_pairs={{0,3},{1,0},{2,1},{3,2},{4,7},{5,4},{6,5},{7,6},{8,11},{9,8},{10,9... | collective-permute-start | bytes 786440 | tf_op jit(solution)/shard_map/ppermute | solution.py:29
  195.2 10.1 %collective-permute-start.42 = (f32[128,512]{1,0:T(8,128)S(1)}, f32[128,512]{1,0:T(8,128)S(1)}, u32[]{:S(2)}, u32[]{:S(2)}) collective-permute-start(f32[128,512]{1,0:T(8,128)S(1)} %collective-permute-done.41), channel_id=1, source_target_pairs={{0,1},{1,2},{2,3},{3,0},{4,5},{5,6},{6,7},{7,4},{8,9},{9,10},{10,1... | collective-permute-start | bytes 786440 | tf_op jit(solution)/shard_map/ppermute | solution.py:24
  197.5 7.8 %collective-permute-start.43 = (f32[128,512]{1,0:T(8,128)S(1)}, f32[128,512]{1,0:T(8,128)S(1)}, u32[]{:S(2)}, u32[]{:S(2)}) collective-permute-start(f32[128,512]{1,0:T(8,128)S(1)} %collective-permute-done.41), channel_id=1, source_target_pairs={{0,3},{1,0},{2,1},{3,2},{4,7},{5,4},{6,5},{7,6},{8,11},{9,8},{10,9... | collective-permute-start | bytes 786440 | tf_op jit(solution)/shard_map/ppermute | solution.py:29
  199.2 8.9 %collective-permute-start.12 = (f32[128,512]{1,0:T(8,128)S(1)}, f32[128,512]{1,0:T(8,128)S(1)}, u32[]{:S(2)}, u32[]{:S(2)}) collective-permute-start(f32[128,512]{1,0:T(8,128)S(1)} %collective-permute-done.10), channel_id=1, source_target_pairs={{0,1},{1,2},{2,3},{3,0},{4,5},{5,6},{6,7},{7,4},{8,9},{9,10},{10,1... | collective-permute-start | bytes 786440 | tf_op jit(solution)/shard_map/ppermute | solution.py:24
  208.8 13.4 %collective-permute-start.14 = (f32[128,512]{1,0:T(8,128)S(1)}, f32[128,512]{1,0:T(8,128)S(1)}, u32[]{:S(2)}, u32[]{:S(2)}) collective-permute-start(f32[128,512]{1,0:T(8,128)S(1)} %convolution_select_fusion.9), channel_id=1, source_target_pairs={{0,16},{4,20},{8,24},{12,28},{16,32},{20,36},{24,40},{28,44},{32,4... | collective-permute-start | bytes 786440 | tf_op jit(solution)/shard_map/ppermute | solution.py:42
  213.6 49.2 %collective-permute-start.46 = (f32[128,512]{1,0:T(8,128)S(1)}, f32[128,512]{1,0:T(8,128)S(1)}, u32[]{:S(2)}, u32[]{:S(2)}) collective-permute-start(f32[128,512]{1,0:T(8,128)S(1)} %convolution_select_fusion.3), channel_id=1, source_target_pairs={{16,0},{20,4},{24,8},{28,12},{32,16},{36,20},{40,24},{44,28},{48,3... | collective-permute-start | bytes 786440 | tf_op jit(solution)/shard_map/ppermute | solution.py:42
  222.2 43.8 %collective-permute-start.15 = (f32[128,512]{1,0:T(8,128)S(1)}, f32[128,512]{1,0:T(8,128)}, u32[]{:S(2)}, u32[]{:S(2)}) collective-permute-start(f32[128,512]{1,0:T(8,128)S(1)} %collective-permute-done.14), channel_id=1, source_target_pairs={{0,1},{1,2},{2,3},{3,0},{4,5},{5,6},{6,7},{7,4},{8,9},{9,10},{10,1... | collective-permute-start | bytes 786440 | tf_op jit(solution)/shard_map/ppermute | solution.py:24
  223.1 7.7 %collective-permute-start.3 = (f32[4,128]{1,0:T(4,128)S(1)}, f32[4,128]{1,0:T(4,128)S(1)}, u32[]{:S(2)}, u32[]{:S(2)}) collective-permute-start(f32[4,128]{1,0:T(4,128)S(1)} %fusion.34), channel_id=1, source_target_pairs={{0,8},{4,12},{8,16},{12,20},{16,24},{20,28},{24,32},{28,36},{32,40... | collective-permute-start | bytes 6152 | tf_op jit(solution)/shard_map/ppermute | solution.py:42
  241.7 25.4 %collective-permute-start.16 = (f32[128,512]{1,0:T(8,128)S(1)}, f32[128,512]{1,0:T(8,128)S(1)}, u32[]{:S(2)}, u32[]{:S(2)}) collective-permute-start(f32[128,512]{1,0:T(8,128)S(1)} %collective-permute-done.14), channel_id=1, source_target_pairs={{0,3},{1,0},{2,1},{3,2},{4,7},{5,4},{6,5},{7,6},{8,11},{9,8},{10,9... | collective-permute-start | bytes 786440 | tf_op jit(solution)/shard_map/ppermute | solution.py:29
  243.7 8.6 %collective-permute-start.8 = (f32[4,128]{1,0:T(4,128)S(1)}, f32[4,128]{1,0:T(4,128)S(1)}, u32[]{:S(2)}, u32[]{:S(2)}) collective-permute-start(f32[4,128]{1,0:T(4,128)S(1)} %fusion.33), channel_id=1, source_target_pairs={{0,16},{4,20},{8,24},{12,28},{16,32},{20,36},{24,40},{28,44},{32,4... | collective-permute-start | bytes 6152 | tf_op jit(solution)/shard_map/ppermute | solution.py:42
  262.7 37.7 %collective-permute-start.47 = (f32[128,512]{1,0:T(8,128)S(1)}, f32[128,512]{1,0:T(8,128)S(1)}, u32[]{:S(2)}, u32[]{:S(2)}) collective-permute-start(f32[128,512]{1,0:T(8,128)S(1)} %collective-permute-done.46), channel_id=1, source_target_pairs={{0,1},{1,2},{2,3},{3,0},{4,5},{5,6},{6,7},{7,4},{8,9},{9,10},{10,1... | collective-permute-start | bytes 786440 | tf_op jit(solution)/shard_map/ppermute | solution.py:24
  262.8 40.3 %collective-permute-start.48 = (f32[128,512]{1,0:T(8,128)S(1)}, f32[128,512]{1,0:T(8,128)S(1)}, u32[]{:S(2)}, u32[]{:S(2)}) collective-permute-start(f32[128,512]{1,0:T(8,128)S(1)} %collective-permute-done.46), channel_id=1, source_target_pairs={{0,3},{1,0},{2,1},{3,2},{4,7},{5,4},{6,5},{7,6},{8,11},{9,8},{10,9... | collective-permute-start | bytes 786440 | tf_op jit(solution)/shard_map/ppermute | solution.py:29
  266.0 7.8 %collective-permute-start.17 = (f32[128,512]{1,0:T(8,128)}, f32[128,512]{1,0:T(8,128)S(1)}, u32[]{:S(2)}, u32[]{:S(2)}) collective-permute-start(f32[128,512]{1,0:T(8,128)} %collective-permute-done.15), channel_id=1, source_target_pairs={{0,1},{1,2},{2,3},{3,0},{4,5},{5,6},{6,7},{7,4},{8,9},{9,10},{10,1... | collective-permute-start | bytes 786440 | tf_op jit(solution)/shard_map/ppermute | solution.py:24
  274.5 26.1 %collective-permute-start.19 = (f32[128,512]{1,0:T(8,128)S(1)}, f32[128,512]{1,0:T(8,128)S(1)}, u32[]{:S(2)}, u32[]{:S(2)}) collective-permute-start(f32[128,512]{1,0:T(8,128)S(1)} %convolution_select_fusion.8), channel_id=1, source_target_pairs={{0,32},{4,36},{8,40},{12,44},{16,48},{20,52},{24,56},{28,60},{32,6... | collective-permute-start | bytes 786440 | tf_op jit(solution)/shard_map/ppermute | solution.py:42
  276.9 13.1 %collective-permute-start.13 = (f32[4,128]{1,0:T(4,128)S(1)}, f32[4,128]{1,0:T(4,128)S(1)}, u32[]{:S(2)}, u32[]{:S(2)}) collective-permute-start(f32[4,128]{1,0:T(4,128)S(1)} %fusion.32), channel_id=1, source_target_pairs={{0,32},{4,36},{8,40},{12,44},{16,48},{20,52},{24,56},{28,60},{32,6... | collective-permute-start | bytes 6152 | tf_op jit(solution)/shard_map/ppermute | solution.py:42
  300.7 10.2 %collective-permute-start.20 = (f32[128,512]{1,0:T(8,128)S(1)}, f32[128,512]{1,0:T(8,128)S(1)}, u32[]{:S(2)}, u32[]{:S(2)}) collective-permute-start(f32[128,512]{1,0:T(8,128)S(1)} %collective-permute-done.19), channel_id=1, source_target_pairs={{0,1},{1,2},{2,3},{3,0},{4,5},{5,6},{6,7},{7,4},{8,9},{9,10},{10,1... | collective-permute-start | bytes 786440 | tf_op jit(solution)/shard_map/ppermute | solution.py:24
  303.2 8.4 %collective-permute-start.21 = (f32[128,512]{1,0:T(8,128)S(1)}, f32[128,512]{1,0:T(8,128)S(1)}, u32[]{:S(2)}, u32[]{:S(2)}) collective-permute-start(f32[128,512]{1,0:T(8,128)S(1)} %collective-permute-done.19), channel_id=1, source_target_pairs={{0,3},{1,0},{2,1},{3,2},{4,7},{5,4},{6,5},{7,6},{8,11},{9,8},{10,9... | collective-permute-start | bytes 786440 | tf_op jit(solution)/shard_map/ppermute | solution.py:29
  319.2 9.1 %collective-permute-start.24 = (f32[128,512]{1,0:T(8,128)S(1)}, f32[128,512]{1,0:T(8,128)S(1)}, u32[]{:S(2)}, u32[]{:S(2)}) collective-permute-start(f32[128,512]{1,0:T(8,128)S(1)} %convolution_select_fusion.7), channel_id=1, source_target_pairs={{0,64},{4,68},{8,72},{12,76},{16,80},{20,84},{24,88},{28,92},{32,9... | collective-permute-start | bytes 786440 | tf_op jit(solution)/shard_map/ppermute | solution.py:42
  323.3 22.4 %collective-permute-start.51 = (f32[128,512]{1,0:T(8,128)S(1)}, f32[128,512]{1,0:T(8,128)}, u32[]{:S(2)}, u32[]{:S(2)}) collective-permute-start(f32[128,512]{1,0:T(8,128)S(1)} %convolution_select_fusion.2), channel_id=1, source_target_pairs={{32,0},{36,4},{40,8},{44,12},{48,16},{52,20},{56,24},{60,28},{64,3... | collective-permute-start | bytes 786440 | tf_op jit(solution)/shard_map/ppermute | solution.py:42
  328.3 20.6 %collective-permute-start.25 = (f32[128,512]{1,0:T(8,128)S(1)}, f32[128,512]{1,0:T(8,128)S(1)}, u32[]{:S(2)}, u32[]{:S(2)}) collective-permute-start(f32[128,512]{1,0:T(8,128)S(1)} %collective-permute-done.24), channel_id=1, source_target_pairs={{0,1},{1,2},{2,3},{3,0},{4,5},{5,6},{6,7},{7,4},{8,9},{9,10},{10,1... | collective-permute-start | bytes 786440 | tf_op jit(solution)/shard_map/ppermute | solution.py:24
  331.8 18.4 %collective-permute-start.26 = (f32[128,512]{1,0:T(8,128)S(1)}, f32[128,512]{1,0:T(8,128)S(1)}, u32[]{:S(2)}, u32[]{:S(2)}) collective-permute-start(f32[128,512]{1,0:T(8,128)S(1)} %collective-permute-done.24), channel_id=1, source_target_pairs={{0,3},{1,0},{2,1},{3,2},{4,7},{5,4},{6,5},{7,6},{8,11},{9,8},{10,9... | collective-permute-start | bytes 786440 | tf_op jit(solution)/shard_map/ppermute | solution.py:29
  345.6 14.8 %collective-permute-start.52 = (f32[128,512]{1,0:T(8,128)}, f32[128,512]{1,0:T(8,128)S(1)}, u32[]{:S(2)}, u32[]{:S(2)}) collective-permute-start(f32[128,512]{1,0:T(8,128)} %collective-permute-done.51), channel_id=1, source_target_pairs={{0,1},{1,2},{2,3},{3,0},{4,5},{5,6},{6,7},{7,4},{8,9},{9,10},{10,1... | collective-permute-start | bytes 786440 | tf_op jit(solution)/shard_map/ppermute | solution.py:24
  348.0 13.2 %collective-permute-start.53 = (f32[128,512]{1,0:T(8,128)}, f32[128,512]{1,0:T(8,128)S(1)}, u32[]{:S(2)}, u32[]{:S(2)}) collective-permute-start(f32[128,512]{1,0:T(8,128)} %collective-permute-done.51), channel_id=1, source_target_pairs={{0,3},{1,0},{2,1},{3,2},{4,7},{5,4},{6,5},{7,6},{8,11},{9,8},{10,9... | collective-permute-start | bytes 786440 | tf_op jit(solution)/shard_map/ppermute | solution.py:29
  360.4 12.3 %collective-permute-start.54 = (f32[128,512]{1,0:T(8,128)S(1)}, f32[128,512]{1,0:T(8,128)S(1)}, u32[]{:S(2)}, u32[]{:S(2)}) collective-permute-start(f32[128,512]{1,0:T(8,128)S(1)} %collective-permute-done.52), channel_id=1, source_target_pairs={{0,1},{1,2},{2,3},{3,0},{4,5},{5,6},{6,7},{7,4},{8,9},{9,10},{10,1... | collective-permute-start | bytes 786440 | tf_op jit(solution)/shard_map/ppermute | solution.py:24
  363.2 20.1 %collective-permute-start.29 = (f32[128,512]{1,0:T(8,128)S(1)}, f32[128,512]{1,0:T(8,128)S(1)}, u32[]{:S(2)}, u32[]{:S(2)}) collective-permute-start(f32[128,512]{1,0:T(8,128)S(1)} %collective-permute-done.28), channel_id=1, source_target_pairs={{0,1},{1,2},{2,3},{3,0},{4,5},{5,6},{6,7},{7,4},{8,9},{9,10},{10,1... | collective-permute-start | bytes 786440 | tf_op jit(solution)/shard_map/ppermute | solution.py:24
  364.0 8.7 %collective-permute-start.23 = (f32[4,128]{1,0:T(4,128)S(1)}, f32[4,128]{1,0:T(4,128)S(1)}, u32[]{:S(2)}, u32[]{:S(2)}) collective-permute-start(f32[4,128]{1,0:T(4,128)S(1)} %fusion.30), channel_id=1, source_target_pairs={{0,128},{4,132},{8,136},{12,140},{16,144},{20,148},{24,152},{28,15... | collective-permute-start | bytes 6152 | tf_op jit(solution)/shard_map/ppermute | solution.py:42
  370.0 16.0 %collective-permute-start.30 = (f32[128,512]{1,0:T(8,128)S(1)}, f32[128,512]{1,0:T(8,128)S(1)}, u32[]{:S(2)}, u32[]{:S(2)}) collective-permute-start(f32[128,512]{1,0:T(8,128)S(1)} %collective-permute-done.28), channel_id=1, source_target_pairs={{0,3},{1,0},{2,1},{3,2},{4,7},{5,4},{6,5},{7,6},{8,11},{9,8},{10,9... | collective-permute-start | bytes 786440 | tf_op jit(solution)/shard_map/ppermute | solution.py:29
  383.3 7.8 %collective-permute-start.31 = (f32[128,512]{1,0:T(8,128)S(1)}, f32[128,512]{1,0:T(8,128)S(1)}, u32[]{:S(2)}, u32[]{:S(2)}) collective-permute-start(f32[128,512]{1,0:T(8,128)S(1)} %collective-permute-done.29), channel_id=1, source_target_pairs={{0,1},{1,2},{2,3},{3,0},{4,5},{5,6},{6,7},{7,4},{8,9},{9,10},{10,1... | collective-permute-start | bytes 786440 | tf_op jit(solution)/shard_map/ppermute | solution.py:24
  393.0 8.4 %all-to-all-start = ((f32[4,1,128]{2,1,0:T(1,128)}), f32[4,1,128]{2,1,0:T(1,128)S(1)}, u32[]{:S(2)}, u32[]{:S(2)}) async-start(f32[4,1,128]{2,1,0:T(1,128)} %bitcast.18), calls=%async_computation | async-start | bytes 4096 | tf_op jit(solution)/shard_map/all_to_all | solution.py:132
  397.0 110.3 %collective-permute-start.56 = (f32[128,512]{1,0:T(8,128)S(1)}, f32[128,512]{1,0:T(8,128)S(1)}, u32[]{:S(2)}, u32[]{:S(2)}) collective-permute-start(f32[128,512]{1,0:T(8,128)S(1)} %convolution_select_fusion.1), channel_id=1, source_target_pairs={{64,0},{68,4},{72,8},{76,12},{80,16},{84,20},{88,24},{92,28},{96,3... | collective-permute-start | bytes 786440 | tf_op jit(solution)/shard_map/ppermute | solution.py:42
  501.5 9.1 %collective-permute-start.33 = (f32[4,128]{1,0:T(4,128)S(1)}, f32[4,128]{1,0:T(4,128)S(1)}, u32[]{:S(2)}, u32[]{:S(2)}) collective-permute-start(f32[4,128]{1,0:T(4,128)S(1)} %broadcast_select_fusion.2), channel_id=1, source_target_pairs={{4,0},{8,4},{12,8},{16,12},{20,16},{24,20},{28,24},{32,28},{36,32}... | collective-permute-start | bytes 6152 | tf_op jit(solution)/shard_map/ppermute | solution.py:42
  507.3 16.3 %collective-permute-start.57 = (f32[128,512]{1,0:T(8,128)S(1)}, f32[128,512]{1,0:T(8,128)S(1)}, u32[]{:S(2)}, u32[]{:S(2)}) collective-permute-start(f32[128,512]{1,0:T(8,128)S(1)} %collective-permute-done.56), channel_id=1, source_target_pairs={{0,1},{1,2},{2,3},{3,0},{4,5},{5,6},{6,7},{7,4},{8,9},{9,10},{10,1... | collective-permute-start | bytes 786440 | tf_op jit(solution)/shard_map/ppermute | solution.py:24
  507.9 50.5 %collective-permute-start.58 = (f32[128,512]{1,0:T(8,128)S(1)}, f32[128,512]{1,0:T(8,128)S(1)}, u32[]{:S(2)}, u32[]{:S(2)}) collective-permute-start(f32[128,512]{1,0:T(8,128)S(1)} %collective-permute-done.56), channel_id=1, source_target_pairs={{0,3},{1,0},{2,1},{3,2},{4,7},{5,4},{6,5},{7,6},{8,11},{9,8},{10,9... | collective-permute-start | bytes 786440 | tf_op jit(solution)/shard_map/ppermute | solution.py:29
  523.5 53.6 %collective-permute-start.59 = (f32[128,512]{1,0:T(8,128)S(1)}, f32[128,512]{1,0:T(8,128)S(1)}, u32[]{:S(2)}, u32[]{:S(2)}) collective-permute-start(f32[128,512]{1,0:T(8,128)S(1)} %collective-permute-done.57), channel_id=1, source_target_pairs={{0,1},{1,2},{2,3},{3,0},{4,5},{5,6},{6,7},{7,4},{8,9},{9,10},{10,1... | collective-permute-start | bytes 786440 | tf_op jit(solution)/shard_map/ppermute | solution.py:24
  555.1 9.5 %collective-permute-start.45 = (f32[4,128]{1,0:T(4,128)S(1)}, f32[4,128]{1,0:T(4,128)S(1)}, u32[]{:S(2)}, u32[]{:S(2)}) collective-permute-start(f32[4,128]{1,0:T(4,128)S(1)} %fusion.25), channel_id=1, source_target_pairs={{32,0},{36,4},{40,8},{44,12},{48,16},{52,20},{56,24},{60,28},{64,3... | collective-permute-start | bytes 6152 | tf_op jit(solution)/shard_map/ppermute | solution.py:42
  (22 other events, 482.3 us)
Sparse Core Ops, SparseCore 0:
  9.8 29.4 all-gather.1
